TPU v7x, 512 devices: a whole 4x4x16 slice. The times are simulated.
512 devices in a mesh: req: 32 (over x, y, core), ctx: 16 (over z).
Axes of the slice: x: 4, y: 4, z: 16, core: 2. Of those that a mesh axis runs over, the one named last changes fastest.
Arguments:
- queries: bfloat16 [64, 48, 8192], P('req', None, 'ctx'), parts along dimension 0, may hold values from -120 to 120
- key_cache: bfloat16 [64, 2048, 1024], P('req', 'ctx'), parts along dimension 0, may hold values from -5 to 5
- value_cache: bfloat16 [64, 2048, 1024], P('req', 'ctx'), parts along dimension 0, may hold values from -6 to 6
- draft_keys: bfloat16 [64, 48, 1024], P('req', None, 'ctx'), parts along dimension 0, may hold values from -12 to 12
- draft_values: bfloat16 [64, 48, 1024], P('req', None, 'ctx'), parts along dimension 0, may hold values from -6 to 6
- ancestors: int32 [64, 24, 24], P('req'), parts along dimension 0, may hold values from 0 to 1, as said below
- context_length: int32 [32], P('req'), parts along dimension 0, may hold values from 1025 to 2048
Outputs:
- attention: float32 [64, 48, 8192], P('req', None, 'ctx'), parts along dimension 0
There are 32 independent parts, one for each index of `req`. A program takes and returns all parts, laid end to end along the dimension named above; each array names one. Nothing has to cross between parts.
Inputs may be any that keep to these rules, and one draw needn't show every extreme that they name: ancestors[t, n, j] is 1 exactly where node j of tree t is node n itself or one of its ancestors; node 0 is the root of every tree and every other node's parent has a lower number.
All inputs are finite; a program needn't handle non-finite values.
Results may differ from a plain program's by a relative error of at most 0.005.
Values may be sent and summed in bfloat16 or wider, within the bound.
No kernel may reach another device: no remote copies, remote signals or barrier semaphores. Data moves between devices by JAX's collectives and lax.ppermute only.
A program may use at most 64 MiB of HBM per device.

v0:
```python
import math
import jax
import jax.numpy as jnp
from jax import lax
from jax.sharding import PartitionSpec as P

H = 64
KVH = 8
DH = 128
masked_score = -1e30


def sent_together(arrays, axis, dim, along):
    ends, at = ([], 0)
    for a in arrays[:-1]:
        at += a.shape[along]
        ends.append(at)
    both = jnp.concatenate(arrays, axis=along)
    return tuple(jnp.split(lax.all_gather(both, axis, axis=dim, tiled=True), ends, axis=along))


def block_partial(
    query_heads, block_keys, block_values, draft_k, draft_v, cache_keep, draft_keep, score_scale
):
    scores = (
        jnp.einsum("qkjd,pkd->kqjp", query_heads, block_keys, preferred_element_type=jnp.float32)
        * score_scale
    )
    draft_scores = (
        jnp.einsum("qkjd,tkd->kqjt", query_heads, draft_k, preferred_element_type=jnp.float32)
        * score_scale
    )
    scores = jnp.where(cache_keep[None, None, None, :], scores, masked_score)
    draft_scores = jnp.where(draft_keep[None, :, None, :], draft_scores, masked_score)
    top_score = jnp.maximum(jnp.max(scores, -1), jnp.max(draft_scores, -1))
    shift_by = jnp.where(top_score > -1e29, top_score, 0.0)
    cache_weight = jnp.exp(scores - shift_by[..., None])
    draft_weight = jnp.exp(draft_scores - shift_by[..., None])
    total = jnp.sum(cache_weight, -1) + jnp.sum(draft_weight, -1)
    weighted = jnp.einsum(
        "kqjp,pkd->qkjd",
        cache_weight.astype(jnp.bfloat16),
        block_values,
        preferred_element_type=jnp.float32,
    )
    weighted = weighted + jnp.einsum(
        "kqjt,tkd->qkjd",
        draft_weight.astype(jnp.bfloat16),
        draft_v,
        preferred_element_type=jnp.float32,
    )
    top_score = jnp.transpose(top_score, (1, 0, 2))
    total = jnp.transpose(total, (1, 0, 2))
    alive = total > 0.0
    safe_total = jnp.where(alive, total, 1.0)
    output = jnp.where(alive[..., None], weighted / safe_total[..., None], 0.0).astype(jnp.bfloat16)
    lse = jnp.where(alive, top_score + jnp.log(safe_total), masked_score)
    return (lse, output)


def body(queries, key_cache, value_cache, draft_keys, draft_values, ancestors, context_length):
    devices = lax.axis_size("ctx")
    device_index = lax.axis_index("ctx")
    gathered_q, gathered_k, gathered_v = (
        lax.all_gather(queries, "ctx", axis=2, tiled=True),
        *sent_together((draft_keys, draft_values), "ctx", 2, 0),
    )
    layers = gathered_q.shape[0]
    rows = gathered_q.shape[1]
    local_len = key_cache.shape[1]
    trees = ancestors.shape[0]
    group_size = H // KVH
    score_scale = 1.0 / math.sqrt(DH)
    heads_here = H // devices
    tree_keep = (
        jnp.eye(trees, dtype=jnp.int32)[:, None, :, None] * ancestors[:, :, None, :]
    ).reshape(rows, rows) > 0
    draft_keep = jnp.logical_and(tree_keep, device_index == 0)
    cache_keep = (
        device_index * local_len + jnp.arange(local_len, dtype=jnp.int32) < context_length[0]
    )
    results = []
    for layer_index in range(layers):
        query_heads = gathered_q[layer_index].reshape(rows, KVH, group_size, DH)
        lse, output = block_partial(
            query_heads,
            key_cache[layer_index].reshape(local_len, KVH, DH),
            value_cache[layer_index].reshape(local_len, KVH, DH),
            gathered_k[layer_index].reshape(rows, KVH, DH),
            gathered_v[layer_index].reshape(rows, KVH, DH),
            cache_keep,
            draft_keep,
            score_scale,
        )
        lse = lse.reshape(rows, H)
        output = output.reshape(rows, H, DH).astype(jnp.float32)
        lses, outputs = (
            lax.all_to_all(lse[None], "ctx", split_axis=2, concat_axis=0, tiled=True),
            lax.all_to_all(output[None], "ctx", split_axis=2, concat_axis=0, tiled=True),
        )
        overall = jnp.max(lses, 0)
        factor = jnp.exp(lses - overall)
        total_mine = jnp.sum(factor, 0)
        weighted_mine = jnp.sum(factor[..., None] * outputs, 0)
        mine = weighted_mine / total_mine[..., None]
        results.append(mine.reshape(rows, heads_here * DH))
    return jnp.stack(results)


def solution(mesh):
    placed = (
        P("req", None, "ctx"),
        P("req", "ctx", None),
        P("req", "ctx", None),
        P("req", None, "ctx"),
        P("req", None, "ctx"),
        P("req", None, None),
        P("req"),
    )
    return jax.shard_map(
        body, mesh=mesh, in_specs=placed, out_specs=P("req", None, "ctx"), check_vma=False
    )
```

profile of v0, /device:TPU:60, one launch (start us, length us, event | category | flops | bytes accessed | tf_op | source)
XLA Modules:
  0.0 297.8 jit_solution(13309664191307874075)
XLA Ops:
  15.1 42.9 %all_gather.7 = bf16[4,48,1024]{1,0,2:T(4,128)(2,1)S(1)} all-gather(bf16[4,48,64]{1,0,2:T(4,128)(2,1)S(1)} %pad_maximum_fusion.1), channel_id=1, replica_groups=mesh['req'=32,'ctx'=16] {'ctx'}, dimensions={2}, use_global_device_ids=true | all-gather | bytes 417792 | tf_op jit(solution)/shard_map/all_gather | solution.py:19
  58.0 2.2 fusion.34
  62.5 22.9 %all-gather.2.cloned.1.call-done = bf16[2,48,8192]{2,1,0:T(8,128)(2,1)} async-done(((bf16[2,48,512]{2,1,0:T(8,128)(2,1)}), bf16[2,48,8192]{2,1,0:T(8,128)(2,1)}) %all-gather.2.cloned.1.call-update) | async-done | bytes 1572880 | tf_op jit(solution)/shard_map/all_gather | solution.py:65
  85.5 1.5 slice_bitcast_fusion.1
  87.3 2.2 fusion.40
  89.7 1.6 fusion.39
  91.4 2.7 fusion.11
  95.2 1.8 fusion.18
  99.9 8.3 %all-to-all-start = ((f32[16,1,192]{2,1,0:T(1,128)}), f32[16,1,192]{2,1,0:T(1,128)S(1)}, u32[]{:S(2)}, u32[]{:S(2)}) async-start(f32[16,1,192]{2,1,0:T(1,128)} %reshape.145), calls=%async_computation | async-start | bytes 32768 | tf_op jit(solution)/shard_map/all_to_all | solution.py:98
  108.1 2.2 fusion.38
  111.2 2.7 fusion.15
  119.4 11.3 %all-to-all-start.2 = ((f32[16,1,192]{2,1,0:T(1,128)}), f32[16,1,192]{2,1,0:T(1,128)S(1)}, u32[]{:S(2)}, u32[]{:S(2)}) async-start(f32[16,1,192]{2,1,0:T(1,128)} %reshape.143), calls=%async_computation.2 | async-start | bytes 32768 | tf_op jit(solution)/shard_map/all_to_all | solution.py:98
  130.7 2.3 fusion.6
  133.2 2.1 copy.142
  135.3 6.8 %all-to-all-done.2 = f32[16,1,192]{2,1,0:T(1,128)S(1)} async-done(((f32[16,1,192]{2,1,0:T(1,128)}), f32[16,1,192]{2,1,0:T(1,128)S(1)}, u32[]{:S(2)}, u32[]{:S(2)}) %all-to-all-start.2) | async-done | bytes 12320 | tf_op jit(solution)/shard_map/all_to_all | solution.py:98
  142.7 5.2 %all-to-all-start.1 = ((f32[1,48,64,128]{3,1,0,2:T(8,128)}), f32[1,48,64,128]{3,1,0,2:T(8,128)S(1)}, u32[]{:S(2)}, u32[]{:S(2)}) async-start(f32[1,48,64,128]{3,1,0,2:T(8,128)} %copy.142), calls=%async_computation.1 | async-start | bytes 3145728 | tf_op jit(solution)/shard_map/all_to_all | solution.py:99
  147.9 1.8 copy.190
  150.9 2.4 copy.159
  153.3 1.6 fusion.16
  155.0 1.5 fusion.7
  156.7 2.1 copy.161
  158.8 49.8 %all-to-all-done.1 = f32[1,48,64,128]{3,1,0,2:T(8,128)S(1)} async-done(((f32[1,48,64,128]{3,1,0,2:T(8,128)}), f32[1,48,64,128]{3,1,0,2:T(8,128)S(1)}, u32[]{:S(2)}, u32[]{:S(2)}) %all-to-all-start.1) | async-done | bytes 1572896 | tf_op jit(solution)/shard_map/all_to_all | solution.py:99
  208.6 10.4 %all-to-all-start.3 = ((f32[1,48,64,128]{3,1,0,2:T(8,128)}), f32[1,48,64,128]{3,1,0,2:T(8,128)S(1)}, u32[]{:S(2)}, u32[]{:S(2)}) async-start(f32[1,48,64,128]{3,1,0,2:T(8,128)} %copy.161), calls=%async_computation.3 | async-start | bytes 3145728 | tf_op jit(solution)/shard_map/all_to_all | solution.py:99
  221.5 68.1 %all-to-all-done.3 = f32[1,48,64,128]{3,1,0,2:T(8,128)S(1)} async-done(((f32[1,48,64,128]{3,1,0,2:T(8,128)}), f32[1,48,64,128]{3,1,0,2:T(8,128)S(1)}, u32[]{:S(2)}, u32[]{:S(2)}) %all-to-all-start.3) | async-done | bytes 1572896 | tf_op jit(solution)/shard_map/all_to_all | solution.py:99
  (100 shorter events, 26.9 us)
Async XLA Ops:
  6.5 6.9 %copy-start.4 = (bf16[2,128,1024]{2,1,0:T(8,128)(2,1)S(1)}, bf16[2,128,1024]{2,1,0:T(8,128)(2,1)}, u32[]{:S(2)}) copy-start(bf16[2,128,1024]{2,1,0:T(8,128)(2,1)} %param.9) | copy-start | bytes 1572868
  6.5 78.9 %all-gather.2.cloned.1.call-start = ((), (), s32[]{:S(2)}) async-start(), calls=%async_computation.4 | async-start | bytes 1671168 | tf_op jit(solution)/shard_map/all_gather | solution.py:65
  9.0 78.4 %copy-start.11 = (pred[48,48]{0,1:T(8,128)(4,1)}, pred[48,48]{0,1:T(8,128)(4,1)S(1)}, u32[]{:S(2)}) copy-start(pred[48,48]{0,1:T(8,128)(4,1)S(1)} %copy.125) | copy-start | bytes 6916
  62.5 27.2 %copy-start.15 = (pred[128]{0:T(512)(128)(4,1)}, pred[128]{0:T(512)(128)(4,1)S(1)}, u32[]{:S(2)}) copy-start(pred[128]{0:T(512)(128)(4,1)S(1)} %add_compare_fusion) | copy-start | bytes 388
  94.1 1.1 copy-start.2
  96.9 11.2 %copy-start.5 = (bf16[6,8,8,128]{3,2,1,0:T(8,128)(2,1)S(1)}, bf16[6,8,8,128]{3,2,1,0:T(8,128)(2,1)}, u32[]{:S(2)}) copy-start(bf16[6,8,8,128]{3,2,1,0:T(8,128)(2,1)} %copy.195) | copy-start | bytes 294916
  96.9 11.2 %copy-start.12 = (pred[48,48]{0,1:T(8,128)(4,1)S(1)}, pred[48,48]{0,1:T(8,128)(4,1)}, u32[]{:S(2)}) copy-start(pred[48,48]{0,1:T(8,128)(4,1)} %copy-done.11) | copy-start | bytes 6916
  97.7 12.8 %copy-start.1 = (bf16[1,128,1024]{1,2,0:T(8,128)(2,1)S(1)}, bf16[1,128,1024]{1,2,0:T(8,128)(2,1)}, u32[]{:S(2)}) copy-start(bf16[1,128,1024]{1,2,0:T(8,128)(2,1)} %copy.189) | copy-start | bytes 786436
  97.7 12.8 %copy-start.16 = (pred[128]{0:T(512)(128)(4,1)S(1)}, pred[128]{0:T(512)(128)(4,1)}, u32[]{:S(2)}) copy-start(pred[128]{0:T(512)(128)(4,1)} %copy-done.15) | copy-start | bytes 388
  99.9 19.5 %all-to-all-start = ((f32[16,1,192]{2,1,0:T(1,128)}), f32[16,1,192]{2,1,0:T(1,128)S(1)}, u32[]{:S(2)}, u32[]{:S(2)}) async-start(f32[16,1,192]{2,1,0:T(1,128)} %reshape.145), calls=%async_computation | async-start | bytes 32768 | tf_op jit(solution)/shard_map/all_to_all | solution.py:98
  114.0 1.7 copy-start
  115.0 15.7 %copy-start.6 = (f32[48,8,8]{2,0,1:T(8,128)S(1)}, f32[48,8,8]{2,0,1:T(8,128)}, u32[]{:S(2)}) copy-start(f32[48,8,8]{2,0,1:T(8,128)} %get-tuple-element.8) | copy-start | bytes 36868
  115.7 14.9 %copy-start.8 = (bf16[6,8,8,128]{3,2,1,0:T(8,128)(2,1)S(1)}, bf16[6,8,8,128]{3,2,1,0:T(8,128)(2,1)}, u32[]{:S(2)}) copy-start(bf16[6,8,8,128]{3,2,1,0:T(8,128)(2,1)} %copy.193) | copy-start | bytes 294916
  115.8 14.9 %copy-start.13 = (pred[48,8,8]{2,0,1:T(8,128)(4,1)S(1)}, pred[48,8,8]{2,0,1:T(8,128)(4,1)}, u32[]{:S(2)}) copy-start(pred[48,8,8]{2,0,1:T(8,128)(4,1)} %get-tuple-element.9) | copy-start | bytes 9220
  119.4 22.7 %all-to-all-start.2 = ((f32[16,1,192]{2,1,0:T(1,128)}), f32[16,1,192]{2,1,0:T(1,128)S(1)}, u32[]{:S(2)}, u32[]{:S(2)}) async-start(f32[16,1,192]{2,1,0:T(1,128)} %reshape.143), calls=%async_computation.2 | async-start | bytes 32768 | tf_op jit(solution)/shard_map/all_to_all | solution.py:98
  142.1 0.6 copy-start.9
  142.7 65.9 %all-to-all-start.1 = ((f32[1,48,64,128]{3,1,0,2:T(8,128)}), f32[1,48,64,128]{3,1,0,2:T(8,128)S(1)}, u32[]{:S(2)}, u32[]{:S(2)}) async-start(f32[1,48,64,128]{3,1,0,2:T(8,128)} %copy.142), calls=%async_computation.1 | async-start | bytes 3145728 | tf_op jit(solution)/shard_map/all_to_all | solution.py:99
  153.3 1.6 copy-start.3
  153.3 1.6 copy-start.7
  153.3 1.7 copy-start.14
  158.8 61.0 %copy-start.10 = (f32[16,1,192]{2,1,0:T(1,128)S(1)}, f32[16,1,192]{2,1,0:T(1,128)}, u32[]{:S(2)}) copy-start(f32[16,1,192]{2,1,0:T(1,128)} %copy-done.9) | copy-start | bytes 36868
  208.6 80.9 %all-to-all-start.3 = ((f32[1,48,64,128]{3,1,0,2:T(8,128)}), f32[1,48,64,128]{3,1,0,2:T(8,128)S(1)}, u32[]{:S(2)}, u32[]{:S(2)}) async-start(f32[1,48,64,128]{3,1,0,2:T(8,128)} %copy.161), calls=%async_computation.3 | async-start | bytes 3145728 | tf_op jit(solution)/shard_map/all_to_all | solution.py:99
Sparse Core Ops, SparseCore 0:
  9.4 75.9 all-gather.1
where the time goes:
time: 299 us; the launch traced here: 298 us
  waiting for transfers between devices  149 us (50%)
  blocking collectives  42.9 us (14%)
  starting transfers between devices  35.1 us (12%)
  local copies, waits for them, and re-layouts  27.5 us (9%)
  other arithmetic  14.7 us (5%)
  between operations  14.5 us (5%)
  matrix products  13.9 us (5%)
    all_to_all x2, waiting for transfers between devices, body(): lax.all_to_all(output[None], 'ctx', split_axis=2, concat_axis=0, tiled=True)  118 us
    all_gather x1, blocking collectives, sent_together(): lax.all_gather(both, axis, axis=dim, tiled=True)  42.9 us
    all_gather x1, waiting for transfers between devices, body(): lax.all_gather(queries, 'ctx', axis=2, tiled=True)  22.9 us
    all_to_all x2, starting transfers between devices, body(): lax.all_to_all(lse[None], 'ctx', split_axis=2, concat_axis=0, tiled=True)  19.5 us
    all_to_all x2, starting transfers between devices, body(): lax.all_to_all(output[None], 'ctx', split_axis=2, concat_axis=0, tiled=True)  15.6 us
    unnamed x52, local copies, waits for them, and re-layouts  12 us
    all_to_all x2, waiting for transfers between devices, body(): lax.all_to_all(lse[None], 'ctx', split_axis=2, concat_axis=0, tiled=True)  7.55 us
    reduce_sum x4, other arithmetic, block_partial(): total = jnp.sum(cache_weight, -1) + jnp.sum(draft_weight, -1)  7.23 us
  transfers between devices with their start and end apart: 5, of which 5 were waited for; matrix products, arithmetic and copies ran while one was open for 13% of the time, Pallas kernels for 0%

commit v1 on v0

--- a/solution.py
+++ b/solution.py
@@ -62,7 +62,9 @@
     devices = lax.axis_size("ctx")
     device_index = lax.axis_index("ctx")
     gathered_q, gathered_k, gathered_v = (
-        lax.all_gather(queries, "ctx", axis=2, tiled=True),
+        jnp.concatenate(
+            lax.all_to_all(jnp.stack([queries] * lax.axis_size("ctx")), "ctx", 0, 0), axis=2
+        ),
         *sent_together((draft_keys, draft_values), "ctx", 2, 0),
     )
     layers = gathered_q.shape[0]

time: 299 us -> 336 us (1.12)
  the two profiles are of different devices: /device:TPU:60 before, /device:TPU:8 now
where the time goes in v1:
time: 336 us
  waiting for transfers between devices  135 us (40%)
  blocking collectives  95.9 us (29%)
  starting transfers between devices  47.9 us (14%)
  local copies, waits for them, and re-layouts  27.3 us (8%)
  other arithmetic  14 us (4%)
  matrix products  13.9 us (4%)
    all_to_all x2, waiting for transfers between devices, body(): lax.all_to_all(output[None], 'ctx', split_axis=2, concat_axis=0, tiled=True)  125 us
    all_gather x1, blocking collectives, sent_together(): lax.all_gather(both, axis, axis=dim, tiled=True)  95.9 us
    all_to_all x2, starting transfers between devices, body(): lax.all_to_all(lse[None], 'ctx', split_axis=2, concat_axis=0, tiled=True)  19.8 us
    all_to_all x1, starting transfers between devices, body(): lax.all_to_all(jnp.stack([queries] * lax.axis_size('ctx')), 'ctx', 0, 0)  15.3 us
    all_to_all x2, starting transfers between devices, body(): lax.all_to_all(output[None], 'ctx', split_axis=2, concat_axis=0, tiled=True)  12.8 us
    all_to_all x2, waiting for transfers between devices, body(): lax.all_to_all(lse[None], 'ctx', split_axis=2, concat_axis=0, tiled=True)  9.87 us
    unnamed x57, local copies, waits for them, and re-layouts  8.75 us
    reduce_sum x4, other arithmetic, block_partial(): total = jnp.sum(cache_weight, -1) + jnp.sum(draft_weight, -1)  7.23 us
  transfers between devices with their start and end apart: 5, of which 4 were waited for; matrix products, arithmetic and copies ran while one was open for 11% of the time, Pallas kernels for 0%

profile of v1, /device:TPU:8, one launch (start us, length us, event | category | flops | bytes accessed | tf_op | source)
XLA Modules:
  0.0 335.6 jit_solution(12616410748228676662)
XLA Ops:
  0.0 2.2 stack.4
  2.2 15.3 %all-to-all-start = ((bf16[16,2,48,512]{3,2,1,0:T(8,128)(2,1)}), bf16[16,2,48,512]{3,2,1,0:T(8,128)(2,1)S(1)}, u32[]{:S(2)}, u32[]{:S(2)}) async-start(bf16[16,2,48,512]{3,2,1,0:T(8,128)(2,1)} %stack.4), calls=%async_computation | async-start | bytes 3145728 | tf_op jit(solution)/shard_map/all_to_all | solution.py:66
  22.3 95.9 %all_gather.3 = bf16[4,48,1024]{1,0,2:T(4,128)(2,1)S(1)} all-gather(bf16[4,48,64]{1,0,2:T(4,128)(2,1)S(1)} %pad_maximum_fusion.1), channel_id=1, replica_groups=mesh['req'=32,'ctx'=16] {'ctx'}, dimensions={2}, use_global_device_ids=true | all-gather | bytes 417792 | tf_op jit(solution)/shard_map/all_gather | solution.py:19
  118.2 2.2 fusion.35
  124.7 2.2 fusion.39
  127.1 1.6 fusion.38
  128.8 2.7 fusion.15
  132.5 1.8 fusion.16
  137.2 9.7 %all-to-all-start.3 = ((f32[16,1,192]{2,1,0:T(1,128)}), f32[16,1,192]{2,1,0:T(1,128)S(1)}, u32[]{:S(2)}, u32[]{:S(2)}) async-start(f32[16,1,192]{2,1,0:T(1,128)} %reshape.154), calls=%async_computation.3 | async-start | bytes 32768 | tf_op jit(solution)/shard_map/all_to_all | solution.py:100
  147.0 2.2 fusion.41
  150.1 2.7 fusion.11
  157.5 2.0 all-to-all-done.3
  159.5 10.0 %all-to-all-start.1 = ((f32[16,1,192]{2,1,0:T(1,128)}), f32[16,1,192]{2,1,0:T(1,128)S(1)}, u32[]{:S(2)}, u32[]{:S(2)}) async-start(f32[16,1,192]{2,1,0:T(1,128)} %reshape.156), calls=%async_computation.1 | async-start | bytes 32768 | tf_op jit(solution)/shard_map/all_to_all | solution.py:100
  169.6 2.3 fusion.7
  172.1 2.1 copy.167
  174.2 7.9 %all-to-all-done.1 = f32[16,1,192]{2,1,0:T(1,128)S(1)} async-done(((f32[16,1,192]{2,1,0:T(1,128)}), f32[16,1,192]{2,1,0:T(1,128)S(1)}, u32[]{:S(2)}, u32[]{:S(2)}) %all-to-all-start.1) | async-done | bytes 12320 | tf_op jit(solution)/shard_map/all_to_all | solution.py:100
  182.6 4.2 %all-to-all-start.4 = ((f32[1,48,64,128]{3,1,0,2:T(8,128)}), f32[1,48,64,128]{3,1,0,2:T(8,128)S(1)}, u32[]{:S(2)}, u32[]{:S(2)}) async-start(f32[1,48,64,128]{3,1,0,2:T(8,128)} %copy.167), calls=%async_computation.4 | async-start | bytes 3145728 | tf_op jit(solution)/shard_map/all_to_all | solution.py:101
  186.8 1.8 copy.194
  189.8 2.4 copy.145
  192.2 1.6 fusion.18
  195.6 2.1 copy.147
  197.7 54.5 %all-to-all-done.4 = f32[1,48,64,128]{3,1,0,2:T(8,128)S(1)} async-done(((f32[1,48,64,128]{3,1,0,2:T(8,128)}), f32[1,48,64,128]{3,1,0,2:T(8,128)S(1)}, u32[]{:S(2)}, u32[]{:S(2)}) %all-to-all-start.4) | async-done | bytes 1572896 | tf_op jit(solution)/shard_map/all_to_all | solution.py:101
  252.2 8.7 %all-to-all-start.2 = ((f32[1,48,64,128]{3,1,0,2:T(8,128)}), f32[1,48,64,128]{3,1,0,2:T(8,128)S(1)}, u32[]{:S(2)}, u32[]{:S(2)}) async-start(f32[1,48,64,128]{3,1,0,2:T(8,128)} %copy.147), calls=%async_computation.2 | async-start | bytes 3145728 | tf_op jit(solution)/shard_map/all_to_all | solution.py:101
  263.4 70.8 %all-to-all-done.2 = f32[1,48,64,128]{3,1,0,2:T(8,128)S(1)} async-done(((f32[1,48,64,128]{3,1,0,2:T(8,128)}), f32[1,48,64,128]{3,1,0,2:T(8,128)S(1)}, u32[]{:S(2)}, u32[]{:S(2)}) %all-to-all-start.2) | async-done | bytes 1572896 | tf_op jit(solution)/shard_map/all_to_all | solution.py:101
  (110 shorter events, 25.4 us)
Async XLA Ops:
  2.2 16.1 %copy-start.18 = (s32[2,24,24]{2,1,0:T(8,128)S(1)}, s32[2,24,24]{2,1,0:T(8,128)}, u32[]{:S(2)}) copy-start(s32[2,24,24]{2,1,0:T(8,128)} %param.12) | copy-start | bytes 13828
  2.2 16.4 %copy-start.16 = (bf16[2,48,64]{2,1,0:T(8,128)(2,1)S(1)}, bf16[2,48,64]{2,1,0:T(8,128)(2,1)}, u32[]{:S(2)}) copy-start(bf16[2,48,64]{2,1,0:T(8,128)(2,1)} %param.10) | copy-start | bytes 36868
  2.2 16.5 %copy-start.17 = (bf16[2,48,64]{2,1,0:T(8,128)(2,1)S(1)}, bf16[2,48,64]{2,1,0:T(8,128)(2,1)}, u32[]{:S(2)}) copy-start(bf16[2,48,64]{2,1,0:T(8,128)(2,1)} %param.11) | copy-start | bytes 36868
  2.2 16.6 %copy-start.4 = (bf16[2,128,1024]{2,1,0:T(8,128)(2,1)S(1)}, bf16[2,128,1024]{2,1,0:T(8,128)(2,1)}, u32[]{:S(2)}) copy-start(bf16[2,128,1024]{2,1,0:T(8,128)(2,1)} %param.8) | copy-start | bytes 1572868
  2.2 120.5 %all-to-all-start = ((bf16[16,2,48,512]{3,2,1,0:T(8,128)(2,1)}), bf16[16,2,48,512]{3,2,1,0:T(8,128)(2,1)S(1)}, u32[]{:S(2)}, u32[]{:S(2)}) async-start(bf16[16,2,48,512]{3,2,1,0:T(8,128)(2,1)} %stack.4), calls=%async_computation | async-start | bytes 3145728 | tf_op jit(solution)/shard_map/all_to_all | solution.py:66
  17.6 3.0 copy-start.5
  18.6 106.1 %copy-start.12 = (pred[48,48]{0,1:T(8,128)(4,1)}, pred[48,48]{0,1:T(8,128)(4,1)S(1)}, u32[]{:S(2)}) copy-start(pred[48,48]{0,1:T(8,128)(4,1)S(1)} %copy.130) | copy-start | bytes 6916
  122.7 4.3 %copy-start.19 = (pred[128]{0:T(512)(128)(4,1)}, pred[128]{0:T(512)(128)(4,1)S(1)}, u32[]{:S(2)}) copy-start(pred[128]{0:T(512)(128)(4,1)S(1)} %add_compare_fusion) | copy-start | bytes 388
  134.3 12.7 %copy-start.6 = (bf16[6,8,8,128]{3,2,1,0:T(8,128)(2,1)S(1)}, bf16[6,8,8,128]{3,2,1,0:T(8,128)(2,1)}, u32[]{:S(2)}) copy-start(bf16[6,8,8,128]{3,2,1,0:T(8,128)(2,1)} %copy.197) | copy-start | bytes 294916
  134.3 12.7 %copy-start.13 = (pred[48,48]{0,1:T(8,128)(4,1)S(1)}, pred[48,48]{0,1:T(8,128)(4,1)}, u32[]{:S(2)}) copy-start(pred[48,48]{0,1:T(8,128)(4,1)} %copy-done.12) | copy-start | bytes 6916
  135.1 14.3 %copy-start.1 = (bf16[1,128,1024]{1,2,0:T(8,128)(2,1)S(1)}, bf16[1,128,1024]{1,2,0:T(8,128)(2,1)}, u32[]{:S(2)}) copy-start(bf16[1,128,1024]{1,2,0:T(8,128)(2,1)} %copy.193) | copy-start | bytes 786436
  135.1 14.3 %copy-start.20 = (pred[128]{0:T(512)(128)(4,1)S(1)}, pred[128]{0:T(512)(128)(4,1)}, u32[]{:S(2)}) copy-start(pred[128]{0:T(512)(128)(4,1)} %copy-done.19) | copy-start | bytes 388
  137.2 22.3 %all-to-all-start.3 = ((f32[16,1,192]{2,1,0:T(1,128)}), f32[16,1,192]{2,1,0:T(1,128)S(1)}, u32[]{:S(2)}, u32[]{:S(2)}) async-start(f32[16,1,192]{2,1,0:T(1,128)} %reshape.154), calls=%async_computation.3 | async-start | bytes 32768 | tf_op jit(solution)/shard_map/all_to_all | solution.py:100
  152.9 1.7 copy-start
  153.8 15.7 %copy-start.7 = (f32[48,8,8]{2,0,1:T(8,128)S(1)}, f32[48,8,8]{2,0,1:T(8,128)}, u32[]{:S(2)}) copy-start(f32[48,8,8]{2,0,1:T(8,128)} %get-tuple-element.13) | copy-start | bytes 36868
  154.6 14.9 %copy-start.9 = (bf16[6,8,8,128]{3,2,1,0:T(8,128)(2,1)S(1)}, bf16[6,8,8,128]{3,2,1,0:T(8,128)(2,1)}, u32[]{:S(2)}) copy-start(bf16[6,8,8,128]{3,2,1,0:T(8,128)(2,1)} %copy.200) | copy-start | bytes 294916
  154.6 14.9 %copy-start.14 = (pred[48,8,8]{2,0,1:T(8,128)(4,1)S(1)}, pred[48,8,8]{2,0,1:T(8,128)(4,1)}, u32[]{:S(2)}) copy-start(pred[48,8,8]{2,0,1:T(8,128)(4,1)} %get-tuple-element.14) | copy-start | bytes 9220
  159.5 22.5 %all-to-all-start.1 = ((f32[16,1,192]{2,1,0:T(1,128)}), f32[16,1,192]{2,1,0:T(1,128)S(1)}, u32[]{:S(2)}, u32[]{:S(2)}) async-start(f32[16,1,192]{2,1,0:T(1,128)} %reshape.156), calls=%async_computation.1 | async-start | bytes 32768 | tf_op jit(solution)/shard_map/all_to_all | solution.py:100
  182.6 69.6 %all-to-all-start.4 = ((f32[1,48,64,128]{3,1,0,2:T(8,128)}), f32[1,48,64,128]{3,1,0,2:T(8,128)S(1)}, u32[]{:S(2)}, u32[]{:S(2)}) async-start(f32[1,48,64,128]{3,1,0,2:T(8,128)} %copy.167), calls=%async_computation.4 | async-start | bytes 3145728 | tf_op jit(solution)/shard_map/all_to_all | solution.py:101
  192.2 1.6 copy-start.3
  192.2 1.6 copy-start.8
  192.2 1.7 copy-start.15
  197.7 64.1 %copy-start.11 = (f32[16,1,192]{2,1,0:T(1,128)S(1)}, f32[16,1,192]{2,1,0:T(1,128)}, u32[]{:S(2)}) copy-start(f32[16,1,192]{2,1,0:T(1,128)} %copy-done.10) | copy-start | bytes 36868
  252.2 82.0 %all-to-all-start.2 = ((f32[1,48,64,128]{3,1,0,2:T(8,128)}), f32[1,48,64,128]{3,1,0,2:T(8,128)S(1)}, u32[]{:S(2)}, u32[]{:S(2)}) async-start(f32[1,48,64,128]{3,1,0,2:T(8,128)} %copy.147), calls=%async_computation.2 | async-start | bytes 3145728 | tf_op jit(solution)/shard_map/all_to_all | solution.py:101
  (2 other events, 1.7 us)
